TPU v7x, 256 devices: a whole 4x4x8 slice. The times are simulated.
256 devices in a mesh: run: 2 (over core), ctx: 32 (over x, z), head: 4 (over y).
Axes of the slice: x: 4, y: 4, z: 8, core: 2. Of those that a mesh axis runs over, the one named last changes fastest.
Arguments:
- inner_tokens: bfloat16 [131072, 5120], P(('run', 'ctx', 'head')), parts along dimension 0, may hold values from -6 to 6
- state_inputs: bfloat16 [131072, 256], P(('run', 'ctx', 'head')), parts along dimension 0, may hold values from -6 to 6
- step_raw: bfloat16 [131072, 80], P(('run', 'ctx', 'head')), parts along dimension 0, may hold values from -3 to 24
- conv_inner: float32 [5, 5120], P(None, 'head'), may hold values from -3 to 3
- conv_state: float32 [5, 256], replicated, may hold values from -3 to 3
- head_rates: float32 [4, 80], P('run', 'head'), parts along dimension 0, may hold values from -15 to 4
- skip_gain: float32 [80], P('head'), may hold values from 0.5 to 1.5
Outputs:
- mixed: bfloat16 [131072, 5120], P(('run', 'ctx', 'head')), parts along dimension 0
There are 2 independent parts, one for each index of `run`. A program takes and returns all parts, laid end to end along the dimension named above; an argument that names none is the same for every part. Nothing has to cross between parts.
All inputs are finite; a program needn't handle non-finite values.
Results may differ from a plain program's by a relative error of at most 0.009.
Values may be sent and summed in bfloat16 or wider, within the bound.
No kernel may reach another device: no remote copies, remote signals or barrier semaphores. Data moves between devices by JAX's collectives and lax.ppermute only.
A program may use at most 192 MiB of HBM per device.

v0:
```python
import jax
import jax.numpy as jnp
from jax import lax
from jax.sharding import PartitionSpec as P

KERNEL = 4
SPAN = 256


def from_behind(value, axis, by):
    length = lax.axis_size(axis)
    pairs = [(i, i + by) for i in range(length) if 0 <= i + by < length]
    return lax.ppermute(value, axis, pairs)


def silu_conv(signal, previous_rows, kernel_taps):
    length = signal.shape[0]
    channels = signal.shape[1]
    padded = jnp.concatenate(
        [previous_rows.astype(jnp.float32), signal.astype(jnp.float32)], axis=0
    )
    summed = jnp.zeros((length, channels), jnp.float32) + kernel_taps[KERNEL][None, :]
    for offset in range(KERNEL):
        summed = summed + kernel_taps[offset][None, :] * padded[offset : offset + length]
    return jax.nn.silu(summed).astype(jnp.bfloat16)


def block_terms(carry_state, pieces):
    c_block, b_block, u_block, decay_block = pieces
    cumulative = jnp.cumsum(decay_block, axis=0)
    across = cumulative.T
    inner_scores = jnp.dot(c_block, b_block.T, preferred_element_type=jnp.float32)
    spread = across[:, :, None] - across[:, None, :]
    places = jnp.arange(c_block.shape[0])
    causal = places[:, None] >= places[None, :]
    mixing = (inner_scores[None] * jnp.exp(jnp.where(causal[None], spread, -jnp.inf))).astype(
        jnp.bfloat16
    )
    local_terms = jnp.einsum("hts,shp->thp", mixing, u_block, preferred_element_type=jnp.float32)
    carried = jnp.exp(cumulative)[:, :, None] * jnp.einsum(
        "tn,hpn->thp", c_block.astype(jnp.float32), carry_state, precision=lax.Precision.HIGHEST
    )
    ending = cumulative[-1]
    weights = jnp.exp(ending[None, :] - cumulative)
    scaled = weights[:, :, None] * u_block.astype(jnp.float32)
    new_state = jnp.exp(ending)[:, None, None] * carry_state + jnp.einsum(
        "shp,sn->hpn", scaled, b_block.astype(jnp.float32), precision=lax.Precision.HIGHEST
    )
    return (new_state, local_terms + carried)


def per_device(inner_tokens, state_inputs, step_raw, conv_inner, conv_state, head_rates, skip_gain):
    x_local, step_local = (
        lax.all_to_all(inner_tokens, "head", split_axis=1, concat_axis=0, tiled=True),
        lax.all_to_all(step_raw, "head", split_axis=1, concat_axis=0, tiled=True),
    )
    context = x_local.shape[0]
    channels = x_local.shape[1]
    heads_local = head_rates.shape[1]
    head_width = channels // heads_local
    margin_rows = KERNEL - 1
    state_whole = lax.all_gather(state_inputs, "head", axis=0, tiled=True)
    edge_rows = jnp.concatenate(
        [x_local[context - margin_rows :], state_whole[context - margin_rows :]], axis=1
    )
    previous_rows = from_behind(edge_rows, "ctx", 1)
    x_previous = previous_rows[:, :channels]
    state_conv = silu_conv(state_whole, previous_rows[:, channels:], conv_state)
    inner_conv = silu_conv(x_local, x_previous, conv_inner)
    state_width = state_conv.shape[1] // 2
    b_rows = state_conv[:, :state_width]
    c_rows = state_conv[:, state_width:]
    step_size = jax.nn.softplus(step_local.astype(jnp.float32) + head_rates[0][None, :])
    log_decay = -step_size * jnp.exp(head_rates[1])[None, :]
    x_heads = inner_conv.reshape(context, heads_local, head_width)
    inputs = (x_heads.astype(jnp.float32) * step_size[:, :, None]).astype(jnp.bfloat16)
    block_count = context // SPAN
    start_state = jnp.zeros((heads_local, head_width, state_width), jnp.float32)
    final_state, outputs = lax.scan(
        block_terms,
        start_state,
        (
            c_rows.reshape(block_count, SPAN, state_width),
            b_rows.reshape(block_count, SPAN, state_width),
            inputs.reshape(block_count, SPAN, heads_local, head_width),
            log_decay.reshape(block_count, SPAN, heads_local),
        ),
    )
    running = jnp.cumsum(log_decay, axis=0)
    device_decay = jnp.exp(running[-1])

    def relay(position, arriving):
        return from_behind(device_decay[:, None, None] * arriving + final_state, "ctx", 1)

    incoming = lax.fori_loop(0, lax.axis_size("ctx") - 1, relay, jnp.zeros_like(final_state))
    carried = jnp.exp(running)[:, :, None] * jnp.einsum(
        "tn,hpn->thp", c_rows.astype(jnp.float32), incoming, precision=lax.Precision.HIGHEST
    )
    summed = (
        outputs.reshape(context, heads_local, head_width)
        + carried
        + skip_gain[None, :, None] * x_heads.astype(jnp.float32)
    )
    regrouped = summed.astype(jnp.bfloat16).reshape(context, channels)
    return lax.all_to_all(regrouped, "head", split_axis=0, concat_axis=1, tiled=True)


def solution(mesh):
    return jax.shard_map(
        per_device,
        mesh=mesh,
        in_specs=(
            P(("run", "ctx", "head"), None),
            P(("run", "ctx", "head"), None),
            P(("run", "ctx", "head"), None),
            P(None, "head"),
            P(),
            P("run", "head"),
            P("head"),
        ),
        out_specs=P(("run", "ctx", "head"), None),
        check_vma=False,
    )
```

profile of v0, /device:TPU:6, one launch (start us, length us, event | category | flops | bytes accessed | tf_op | source)
XLA Modules:
  0.0 1098.5 jit_solution(2019038271376231881)
XLA Ops:
  31.9 30.6 %all-gather.2.cloned.1.call-done = bf16[2048,256]{1,0:T(8,128)(2,1)} async-done(((bf16[512,256]{1,0:T(8,128)(2,1)}), bf16[2048,256]{1,0:T(8,128)(2,1)}) %all-gather.2.cloned.1.call-update) | async-done | bytes 1048592 | tf_op jit(solution)/shard_map/all_gather | solution.py:62
  64.6 26.9 %all-to-all-done.1 = bf16[512,4,1280]{2,0,1:T(8,128)(2,1)} async-done(((bf16[512,4,1280]{2,0,1:T(8,128)(2,1)}), bf16[512,4,1280]{2,0,1:T(8,128)(2,1)}, u32[]{:S(2)}, u32[]{:S(2)}) %all-to-all-start.1) | async-done | bytes 5242912 | tf_op jit(solution)/shard_map/all_to_all | solution.py:54
  142.9 307.2 %while.24 = (s32[]{:T(128)}, f32[20,64,128]{2,1,0:T(8,128)S(1)}, f32[8,256,20,64]{1,0,3,2:T(8,128)}, f32[8,256,20]{1,0,2:T(8,128)S(1)}, bf16[8,256,20,64]{1,3,2,...) while((s32[]{:T(128)}, f32[20,64,128]{2,1,0:T(8,128)S(1)}, ...), condition=%wide.region_3.4_spmd.clone, body=%wide.region_0.3_spmd.clone.sunk | while | flops 1199117312 | bytes 13914835 | solution.py:79
  151.5 30.0 %dynamic_update_slice.6 = f32[8,256,20,64]{1,0,3,2:T(8,128)} dynamic-update-slice(f32[8,256,20,64]{1,0,3,2:T(8,128)} %get-tuple-element.251, f32[1,256,20,64]{1,0,3,2:T(1,128)S(1)} %copy.120, s32[]{:T(128)S(6)} %copy.125, s32[]{:T(128)} %constant.36.clone.1..sunk, s32[]{:T(128)} %constant.36.clone.1..sunk, s32[]{:T(128)} %constant.36.clone.1..sunk) | dynamic-update-slice | bytes 2621444 | tf_op jit(solution)/shard_map/while/body/jit(dynamic_update_index_in_dim)/dynamic_update_slice | solution.py:79
  189.9 30.0 %dynamic_update_slice.6 = f32[8,256,20,64]{1,0,3,2:T(8,128)} dynamic-update-slice(f32[8,256,20,64]{1,0,3,2:T(8,128)} %get-tuple-element.251, f32[1,256,20,64]{1,0,3,2:T(1,128)S(1)} %copy.120, s32[]{:T(128)S(6)} %copy.125, s32[]{:T(128)} %constant.36.clone.1..sunk, s32[]{:T(128)} %constant.36.clone.1..sunk, s32[]{:T(128)} %constant.36.clone.1..sunk) | dynamic-update-slice | bytes 2621444 | tf_op jit(solution)/shard_map/while/body/jit(dynamic_update_index_in_dim)/dynamic_update_slice | solution.py:79
  228.2 30.0 %dynamic_update_slice.6 = f32[8,256,20,64]{1,0,3,2:T(8,128)} dynamic-update-slice(f32[8,256,20,64]{1,0,3,2:T(8,128)} %get-tuple-element.251, f32[1,256,20,64]{1,0,3,2:T(1,128)S(1)} %copy.120, s32[]{:T(128)S(6)} %copy.125, s32[]{:T(128)} %constant.36.clone.1..sunk, s32[]{:T(128)} %constant.36.clone.1..sunk, s32[]{:T(128)} %constant.36.clone.1..sunk) | dynamic-update-slice | bytes 2621444 | tf_op jit(solution)/shard_map/while/body/jit(dynamic_update_index_in_dim)/dynamic_update_slice | solution.py:79
  266.6 30.0 %dynamic_update_slice.6 = f32[8,256,20,64]{1,0,3,2:T(8,128)} dynamic-update-slice(f32[8,256,20,64]{1,0,3,2:T(8,128)} %get-tuple-element.251, f32[1,256,20,64]{1,0,3,2:T(1,128)S(1)} %copy.120, s32[]{:T(128)S(6)} %copy.125, s32[]{:T(128)} %constant.36.clone.1..sunk, s32[]{:T(128)} %constant.36.clone.1..sunk, s32[]{:T(128)} %constant.36.clone.1..sunk) | dynamic-update-slice | bytes 2621444 | tf_op jit(solution)/shard_map/while/body/jit(dynamic_update_index_in_dim)/dynamic_update_slice | solution.py:79
  305.0 30.0 %dynamic_update_slice.6 = f32[8,256,20,64]{1,0,3,2:T(8,128)} dynamic-update-slice(f32[8,256,20,64]{1,0,3,2:T(8,128)} %get-tuple-element.251, f32[1,256,20,64]{1,0,3,2:T(1,128)S(1)} %copy.120, s32[]{:T(128)S(6)} %copy.125, s32[]{:T(128)} %constant.36.clone.1..sunk, s32[]{:T(128)} %constant.36.clone.1..sunk, s32[]{:T(128)} %constant.36.clone.1..sunk) | dynamic-update-slice | bytes 2621444 | tf_op jit(solution)/shard_map/while/body/jit(dynamic_update_index_in_dim)/dynamic_update_slice | solution.py:79
  343.3 30.0 %dynamic_update_slice.6 = f32[8,256,20,64]{1,0,3,2:T(8,128)} dynamic-update-slice(f32[8,256,20,64]{1,0,3,2:T(8,128)} %get-tuple-element.251, f32[1,256,20,64]{1,0,3,2:T(1,128)S(1)} %copy.120, s32[]{:T(128)S(6)} %copy.125, s32[]{:T(128)} %constant.36.clone.1..sunk, s32[]{:T(128)} %constant.36.clone.1..sunk, s32[]{:T(128)} %constant.36.clone.1..sunk) | dynamic-update-slice | bytes 2621444 | tf_op jit(solution)/shard_map/while/body/jit(dynamic_update_index_in_dim)/dynamic_update_slice | solution.py:79
  381.7 30.0 %dynamic_update_slice.6 = f32[8,256,20,64]{1,0,3,2:T(8,128)} dynamic-update-slice(f32[8,256,20,64]{1,0,3,2:T(8,128)} %get-tuple-element.251, f32[1,256,20,64]{1,0,3,2:T(1,128)S(1)} %copy.120, s32[]{:T(128)S(6)} %copy.125, s32[]{:T(128)} %constant.36.clone.1..sunk, s32[]{:T(128)} %constant.36.clone.1..sunk, s32[]{:T(128)} %constant.36.clone.1..sunk) | dynamic-update-slice | bytes 2621444 | tf_op jit(solution)/shard_map/while/body/jit(dynamic_update_index_in_dim)/dynamic_update_slice | solution.py:79
  420.1 30.0 %dynamic_update_slice.6 = f32[8,256,20,64]{1,0,3,2:T(8,128)} dynamic-update-slice(f32[8,256,20,64]{1,0,3,2:T(8,128)} %get-tuple-element.251, f32[1,256,20,64]{1,0,3,2:T(1,128)S(1)} %copy.120, s32[]{:T(128)S(6)} %copy.125, s32[]{:T(128)} %constant.36.clone.1..sunk, s32[]{:T(128)} %constant.36.clone.1..sunk, s32[]{:T(128)} %constant.36.clone.1..sunk) | dynamic-update-slice | bytes 2621444 | tf_op jit(solution)/shard_map/while/body/jit(dynamic_update_index_in_dim)/dynamic_update_slice | solution.py:79
  461.6 559.1 %while.23 = (s32[]{:T(128)}, f32[20,64,128]{2,1,0:T(8,128)S(1)}, f32[20]{0:T(128)S(1)}, f32[20,64,128]{2,1,0:T(8,128)S(1)}, s32[]{:T(128)}) while((s32[]{:T(128)}, f32[20,64,128]{2,1,0:T(8,128)S(1)}, f32[20]{0:T(128)S(1)}, f32[20,64,128]{2,1,0:T(8,128)S(1)}, s32[]{:T(128)}) %tuple.57), condition=%wide.region_7.8_spmd, body=%wide.region_6.7_spmd.sunk | while | flops 327682 | bytes 4587701 | solution.py:95
  463.8 16.0 %collective-permute-done = f32[20,64,128]{2,1,0:T(8,128)S(1)} collective-permute-done((f32[20,64,128]{2,1,0:T(8,128)S(1)}, f32[20,64,128]{2,1,0:T(8,128)S(1)}, u32[]{:S(2)}, u32[]{:S(2)}) %collective-permute-start) | collective-permute-done | bytes 655392 | tf_op jit(solution)/shard_map/while/body/eval_jaxpr/ppermute | solution.py:13
  562.5 15.5 %collective-permute-done = f32[20,64,128]{2,1,0:T(8,128)S(1)} collective-permute-done((f32[20,64,128]{2,1,0:T(8,128)S(1)}, f32[20,64,128]{2,1,0:T(8,128)S(1)}, u32[]{:S(2)}, u32[]{:S(2)}) %collective-permute-start) | collective-permute-done | bytes 655392 | tf_op jit(solution)/shard_map/while/body/eval_jaxpr/ppermute | solution.py:13
  580.1 16.7 %collective-permute-done = f32[20,64,128]{2,1,0:T(8,128)S(1)} collective-permute-done((f32[20,64,128]{2,1,0:T(8,128)S(1)}, f32[20,64,128]{2,1,0:T(8,128)S(1)}, u32[]{:S(2)}, u32[]{:S(2)}) %collective-permute-start) | collective-permute-done | bytes 655392 | tf_op jit(solution)/shard_map/while/body/eval_jaxpr/ppermute | solution.py:13
  598.9 17.8 %collective-permute-done = f32[20,64,128]{2,1,0:T(8,128)S(1)} collective-permute-done((f32[20,64,128]{2,1,0:T(8,128)S(1)}, f32[20,64,128]{2,1,0:T(8,128)S(1)}, u32[]{:S(2)}, u32[]{:S(2)}) %collective-permute-start) | collective-permute-done | bytes 655392 | tf_op jit(solution)/shard_map/while/body/eval_jaxpr/ppermute | solution.py:13
  618.8 19.0 %collective-permute-done = f32[20,64,128]{2,1,0:T(8,128)S(1)} collective-permute-done((f32[20,64,128]{2,1,0:T(8,128)S(1)}, f32[20,64,128]{2,1,0:T(8,128)S(1)}, u32[]{:S(2)}, u32[]{:S(2)}) %collective-permute-start) | collective-permute-done | bytes 655392 | tf_op jit(solution)/shard_map/while/body/eval_jaxpr/ppermute | solution.py:13
  639.9 19.2 %collective-permute-done = f32[20,64,128]{2,1,0:T(8,128)S(1)} collective-permute-done((f32[20,64,128]{2,1,0:T(8,128)S(1)}, f32[20,64,128]{2,1,0:T(8,128)S(1)}, u32[]{:S(2)}, u32[]{:S(2)}) %collective-permute-start) | collective-permute-done | bytes 655392 | tf_op jit(solution)/shard_map/while/body/eval_jaxpr/ppermute | solution.py:13
  661.1 18.4 %collective-permute-done = f32[20,64,128]{2,1,0:T(8,128)S(1)} collective-permute-done((f32[20,64,128]{2,1,0:T(8,128)S(1)}, f32[20,64,128]{2,1,0:T(8,128)S(1)}, u32[]{:S(2)}, u32[]{:S(2)}) %collective-permute-start) | collective-permute-done | bytes 655392 | tf_op jit(solution)/shard_map/while/body/eval_jaxpr/ppermute | solution.py:13
  681.6 17.5 %collective-permute-done = f32[20,64,128]{2,1,0:T(8,128)S(1)} collective-permute-done((f32[20,64,128]{2,1,0:T(8,128)S(1)}, f32[20,64,128]{2,1,0:T(8,128)S(1)}, u32[]{:S(2)}, u32[]{:S(2)}) %collective-permute-start) | collective-permute-done | bytes 655392 | tf_op jit(solution)/shard_map/while/body/eval_jaxpr/ppermute | solution.py:13
  701.1 16.7 %collective-permute-done = f32[20,64,128]{2,1,0:T(8,128)S(1)} collective-permute-done((f32[20,64,128]{2,1,0:T(8,128)S(1)}, f32[20,64,128]{2,1,0:T(8,128)S(1)}, u32[]{:S(2)}, u32[]{:S(2)}) %collective-permute-start) | collective-permute-done | bytes 655392 | tf_op jit(solution)/shard_map/while/body/eval_jaxpr/ppermute | solution.py:13
  719.9 15.8 %collective-permute-done = f32[20,64,128]{2,1,0:T(8,128)S(1)} collective-permute-done((f32[20,64,128]{2,1,0:T(8,128)S(1)}, f32[20,64,128]{2,1,0:T(8,128)S(1)}, u32[]{:S(2)}, u32[]{:S(2)}) %collective-permute-start) | collective-permute-done | bytes 655392 | tf_op jit(solution)/shard_map/while/body/eval_jaxpr/ppermute | solution.py:13
  818.3 15.7 %collective-permute-done = f32[20,64,128]{2,1,0:T(8,128)S(1)} collective-permute-done((f32[20,64,128]{2,1,0:T(8,128)S(1)}, f32[20,64,128]{2,1,0:T(8,128)S(1)}, u32[]{:S(2)}, u32[]{:S(2)}) %collective-permute-start) | collective-permute-done | bytes 655392 | tf_op jit(solution)/shard_map/while/body/eval_jaxpr/ppermute | solution.py:13
  836.0 16.8 %collective-permute-done = f32[20,64,128]{2,1,0:T(8,128)S(1)} collective-permute-done((f32[20,64,128]{2,1,0:T(8,128)S(1)}, f32[20,64,128]{2,1,0:T(8,128)S(1)}, u32[]{:S(2)}, u32[]{:S(2)}) %collective-permute-start) | collective-permute-done | bytes 655392 | tf_op jit(solution)/shard_map/while/body/eval_jaxpr/ppermute | solution.py:13
  855.0 18.0 %collective-permute-done = f32[20,64,128]{2,1,0:T(8,128)S(1)} collective-permute-done((f32[20,64,128]{2,1,0:T(8,128)S(1)}, f32[20,64,128]{2,1,0:T(8,128)S(1)}, u32[]{:S(2)}, u32[]{:S(2)}) %collective-permute-start) | collective-permute-done | bytes 655392 | tf_op jit(solution)/shard_map/while/body/eval_jaxpr/ppermute | solution.py:13
  875.0 19.1 %collective-permute-done = f32[20,64,128]{2,1,0:T(8,128)S(1)} collective-permute-done((f32[20,64,128]{2,1,0:T(8,128)S(1)}, f32[20,64,128]{2,1,0:T(8,128)S(1)}, u32[]{:S(2)}, u32[]{:S(2)}) %collective-permute-start) | collective-permute-done | bytes 655392 | tf_op jit(solution)/shard_map/while/body/eval_jaxpr/ppermute | solution.py:13
  896.2 19.1 %collective-permute-done = f32[20,64,128]{2,1,0:T(8,128)S(1)} collective-permute-done((f32[20,64,128]{2,1,0:T(8,128)S(1)}, f32[20,64,128]{2,1,0:T(8,128)S(1)}, u32[]{:S(2)}, u32[]{:S(2)}) %collective-permute-start) | collective-permute-done | bytes 655392 | tf_op jit(solution)/shard_map/while/body/eval_jaxpr/ppermute | solution.py:13
  917.4 18.2 %collective-permute-done = f32[20,64,128]{2,1,0:T(8,128)S(1)} collective-permute-done((f32[20,64,128]{2,1,0:T(8,128)S(1)}, f32[20,64,128]{2,1,0:T(8,128)S(1)}, u32[]{:S(2)}, u32[]{:S(2)}) %collective-permute-start) | collective-permute-done | bytes 655392 | tf_op jit(solution)/shard_map/while/body/eval_jaxpr/ppermute | solution.py:13
  937.6 17.4 %collective-permute-done = f32[20,64,128]{2,1,0:T(8,128)S(1)} collective-permute-done((f32[20,64,128]{2,1,0:T(8,128)S(1)}, f32[20,64,128]{2,1,0:T(8,128)S(1)}, u32[]{:S(2)}, u32[]{:S(2)}) %collective-permute-start) | collective-permute-done | bytes 655392 | tf_op jit(solution)/shard_map/while/body/eval_jaxpr/ppermute | solution.py:13
  957.0 16.5 %collective-permute-done = f32[20,64,128]{2,1,0:T(8,128)S(1)} collective-permute-done((f32[20,64,128]{2,1,0:T(8,128)S(1)}, f32[20,64,128]{2,1,0:T(8,128)S(1)}, u32[]{:S(2)}, u32[]{:S(2)}) %collective-permute-start) | collective-permute-done | bytes 655392 | tf_op jit(solution)/shard_map/while/body/eval_jaxpr/ppermute | solution.py:13
  975.6 15.6 %collective-permute-done = f32[20,64,128]{2,1,0:T(8,128)S(1)} collective-permute-done((f32[20,64,128]{2,1,0:T(8,128)S(1)}, f32[20,64,128]{2,1,0:T(8,128)S(1)}, u32[]{:S(2)}, u32[]{:S(2)}) %collective-permute-start) | collective-permute-done | bytes 655392 | tf_op jit(solution)/shard_map/while/body/eval_jaxpr/ppermute | solution.py:13
  1046.9 36.9 %all_to_all.51 = bf16[4,512,1280]{1,2,0:T(8,128)(2,1)} all-to-all(bf16[4,512,1280]{1,2,0:T(8,128)(2,1)S(1)} %copy.91), channel_id=1, replica_groups=mesh['run'=2,'ctx'=32,'head'=4] {'head'}, dimensions={0} | all-to-all | bytes 10485760 | tf_op jit(solution)/shard_map/all_to_all | solution.py:105
  (310 shorter events, 419.5 us)
Async XLA Ops:
  18.3 73.1 %all-to-all-start.1 = ((bf16[512,4,1280]{2,0,1:T(8,128)(2,1)}), bf16[512,4,1280]{2,0,1:T(8,128)(2,1)}, u32[]{:S(2)}, u32[]{:S(2)}) async-start(bf16[512,4,1280]{2,0,1:T(8,128)(2,1)} %bitcast.129), calls=%async_computation.1 | async-start | bytes 10485760 | tf_op jit(solution)/shard_map/all_to_all | solution.py:54
  23.5 39.0 %all-gather.2.cloned.1.call-start = ((), (), s32[]{:S(2)}) async-start(), calls=%async_computation.3 | async-start | bytes 1310720 | tf_op jit(solution)/shard_map/all_gather | solution.py:62
  461.7 18.0 %collective-permute-start = (f32[20,64,128]{2,1,0:T(8,128)S(1)}, f32[20,64,128]{2,1,0:T(8,128)S(1)}, u32[]{:S(2)}, u32[]{:S(2)}) collective-permute-start(f32[20,64,128]{2,1,0:T(8,128)S(1)} %multiply_add_fusion.2), channel_id=1, source_target_pairs={{0,4},{4,8},{8,12},{12,16},{16,20},{20,24},{24,28},{28,32},{32,36}... | collective-permute-start | bytes 1966088 | tf_op jit(solution)/shard_map/while/body/eval_jaxpr/ppermute | solution.py:13
  479.9 17.0 %collective-permute-start = (f32[20,64,128]{2,1,0:T(8,128)S(1)}, f32[20,64,128]{2,1,0:T(8,128)S(1)}, u32[]{:S(2)}, u32[]{:S(2)}) collective-permute-start(f32[20,64,128]{2,1,0:T(8,128)S(1)} %multiply_add_fusion.2), channel_id=1, source_target_pairs={{0,4},{4,8},{8,12},{12,16},{16,20},{20,24},{24,28},{28,32},{32,36}... | collective-permute-start | bytes 1966088 | tf_op jit(solution)/shard_map/while/body/eval_jaxpr/ppermute | solution.py:13
  497.1 16.2 %collective-permute-start = (f32[20,64,128]{2,1,0:T(8,128)S(1)}, f32[20,64,128]{2,1,0:T(8,128)S(1)}, u32[]{:S(2)}, u32[]{:S(2)}) collective-permute-start(f32[20,64,128]{2,1,0:T(8,128)S(1)} %multiply_add_fusion.2), channel_id=1, source_target_pairs={{0,4},{4,8},{8,12},{12,16},{16,20},{20,24},{24,28},{28,32},{32,36}... | collective-permute-start | bytes 1966088 | tf_op jit(solution)/shard_map/while/body/eval_jaxpr/ppermute | solution.py:13
  513.4 15.3 %collective-permute-start = (f32[20,64,128]{2,1,0:T(8,128)S(1)}, f32[20,64,128]{2,1,0:T(8,128)S(1)}, u32[]{:S(2)}, u32[]{:S(2)}) collective-permute-start(f32[20,64,128]{2,1,0:T(8,128)S(1)} %multiply_add_fusion.2), channel_id=1, source_target_pairs={{0,4},{4,8},{8,12},{12,16},{16,20},{20,24},{24,28},{28,32},{32,36}... | collective-permute-start | bytes 1966088 | tf_op jit(solution)/shard_map/while/body/eval_jaxpr/ppermute | solution.py:13
  528.8 15.2 %collective-permute-start = (f32[20,64,128]{2,1,0:T(8,128)S(1)}, f32[20,64,128]{2,1,0:T(8,128)S(1)}, u32[]{:S(2)}, u32[]{:S(2)}) collective-permute-start(f32[20,64,128]{2,1,0:T(8,128)S(1)} %multiply_add_fusion.2), channel_id=1, source_target_pairs={{0,4},{4,8},{8,12},{12,16},{16,20},{20,24},{24,28},{28,32},{32,36}... | collective-permute-start | bytes 1966088 | tf_op jit(solution)/shard_map/while/body/eval_jaxpr/ppermute | solution.py:13
  544.1 16.3 %collective-permute-start = (f32[20,64,128]{2,1,0:T(8,128)S(1)}, f32[20,64,128]{2,1,0:T(8,128)S(1)}, u32[]{:S(2)}, u32[]{:S(2)}) collective-permute-start(f32[20,64,128]{2,1,0:T(8,128)S(1)} %multiply_add_fusion.2), channel_id=1, source_target_pairs={{0,4},{4,8},{8,12},{12,16},{16,20},{20,24},{24,28},{28,32},{32,36}... | collective-permute-start | bytes 1966088 | tf_op jit(solution)/shard_map/while/body/eval_jaxpr/ppermute | solution.py:13
  560.6 17.5 %collective-permute-start = (f32[20,64,128]{2,1,0:T(8,128)S(1)}, f32[20,64,128]{2,1,0:T(8,128)S(1)}, u32[]{:S(2)}, u32[]{:S(2)}) collective-permute-start(f32[20,64,128]{2,1,0:T(8,128)S(1)} %multiply_add_fusion.2), channel_id=1, source_target_pairs={{0,4},{4,8},{8,12},{12,16},{16,20},{20,24},{24,28},{28,32},{32,36}... | collective-permute-start | bytes 1966088 | tf_op jit(solution)/shard_map/while/body/eval_jaxpr/ppermute | solution.py:13
  578.2 18.6 %collective-permute-start = (f32[20,64,128]{2,1,0:T(8,128)S(1)}, f32[20,64,128]{2,1,0:T(8,128)S(1)}, u32[]{:S(2)}, u32[]{:S(2)}) collective-permute-start(f32[20,64,128]{2,1,0:T(8,128)S(1)} %multiply_add_fusion.2), channel_id=1, source_target_pairs={{0,4},{4,8},{8,12},{12,16},{16,20},{20,24},{24,28},{28,32},{32,36}... | collective-permute-start | bytes 1966088 | tf_op jit(solution)/shard_map/while/body/eval_jaxpr/ppermute | solution.py:13
  597.0 19.8 %collective-permute-start = (f32[20,64,128]{2,1,0:T(8,128)S(1)}, f32[20,64,128]{2,1,0:T(8,128)S(1)}, u32[]{:S(2)}, u32[]{:S(2)}) collective-permute-start(f32[20,64,128]{2,1,0:T(8,128)S(1)} %multiply_add_fusion.2), channel_id=1, source_target_pairs={{0,4},{4,8},{8,12},{12,16},{16,20},{20,24},{24,28},{28,32},{32,36}... | collective-permute-start | bytes 1966088 | tf_op jit(solution)/shard_map/while/body/eval_jaxpr/ppermute | solution.py:13
  616.9 20.9 %collective-permute-start = (f32[20,64,128]{2,1,0:T(8,128)S(1)}, f32[20,64,128]{2,1,0:T(8,128)S(1)}, u32[]{:S(2)}, u32[]{:S(2)}) collective-permute-start(f32[20,64,128]{2,1,0:T(8,128)S(1)} %multiply_add_fusion.2), channel_id=1, source_target_pairs={{0,4},{4,8},{8,12},{12,16},{16,20},{20,24},{24,28},{28,32},{32,36}... | collective-permute-start | bytes 1966088 | tf_op jit(solution)/shard_map/while/body/eval_jaxpr/ppermute | solution.py:13
  637.9 21.2 %collective-permute-start = (f32[20,64,128]{2,1,0:T(8,128)S(1)}, f32[20,64,128]{2,1,0:T(8,128)S(1)}, u32[]{:S(2)}, u32[]{:S(2)}) collective-permute-start(f32[20,64,128]{2,1,0:T(8,128)S(1)} %multiply_add_fusion.2), channel_id=1, source_target_pairs={{0,4},{4,8},{8,12},{12,16},{16,20},{20,24},{24,28},{28,32},{32,36}... | collective-permute-start | bytes 1966088 | tf_op jit(solution)/shard_map/while/body/eval_jaxpr/ppermute | solution.py:13
  659.2 20.3 %collective-permute-start = (f32[20,64,128]{2,1,0:T(8,128)S(1)}, f32[20,64,128]{2,1,0:T(8,128)S(1)}, u32[]{:S(2)}, u32[]{:S(2)}) collective-permute-start(f32[20,64,128]{2,1,0:T(8,128)S(1)} %multiply_add_fusion.2), channel_id=1, source_target_pairs={{0,4},{4,8},{8,12},{12,16},{16,20},{20,24},{24,28},{28,32},{32,36}... | collective-permute-start | bytes 1966088 | tf_op jit(solution)/shard_map/while/body/eval_jaxpr/ppermute | solution.py:13
  679.6 19.4 %collective-permute-start = (f32[20,64,128]{2,1,0:T(8,128)S(1)}, f32[20,64,128]{2,1,0:T(8,128)S(1)}, u32[]{:S(2)}, u32[]{:S(2)}) collective-permute-start(f32[20,64,128]{2,1,0:T(8,128)S(1)} %multiply_add_fusion.2), channel_id=1, source_target_pairs={{0,4},{4,8},{8,12},{12,16},{16,20},{20,24},{24,28},{28,32},{32,36}... | collective-permute-start | bytes 1966088 | tf_op jit(solution)/shard_map/while/body/eval_jaxpr/ppermute | solution.py:13
  699.2 18.6 %collective-permute-start = (f32[20,64,128]{2,1,0:T(8,128)S(1)}, f32[20,64,128]{2,1,0:T(8,128)S(1)}, u32[]{:S(2)}, u32[]{:S(2)}) collective-permute-start(f32[20,64,128]{2,1,0:T(8,128)S(1)} %multiply_add_fusion.2), channel_id=1, source_target_pairs={{0,4},{4,8},{8,12},{12,16},{16,20},{20,24},{24,28},{28,32},{32,36}... | collective-permute-start | bytes 1966088 | tf_op jit(solution)/shard_map/while/body/eval_jaxpr/ppermute | solution.py:13
  717.9 17.7 %collective-permute-start = (f32[20,64,128]{2,1,0:T(8,128)S(1)}, f32[20,64,128]{2,1,0:T(8,128)S(1)}, u32[]{:S(2)}, u32[]{:S(2)}) collective-permute-start(f32[20,64,128]{2,1,0:T(8,128)S(1)} %multiply_add_fusion.2), channel_id=1, source_target_pairs={{0,4},{4,8},{8,12},{12,16},{16,20},{20,24},{24,28},{28,32},{32,36}... | collective-permute-start | bytes 1966088 | tf_op jit(solution)/shard_map/while/body/eval_jaxpr/ppermute | solution.py:13
  735.8 16.9 %collective-permute-start = (f32[20,64,128]{2,1,0:T(8,128)S(1)}, f32[20,64,128]{2,1,0:T(8,128)S(1)}, u32[]{:S(2)}, u32[]{:S(2)}) collective-permute-start(f32[20,64,128]{2,1,0:T(8,128)S(1)} %multiply_add_fusion.2), channel_id=1, source_target_pairs={{0,4},{4,8},{8,12},{12,16},{16,20},{20,24},{24,28},{28,32},{32,36}... | collective-permute-start | bytes 1966088 | tf_op jit(solution)/shard_map/while/body/eval_jaxpr/ppermute | solution.py:13
  752.8 16.0 %collective-permute-start = (f32[20,64,128]{2,1,0:T(8,128)S(1)}, f32[20,64,128]{2,1,0:T(8,128)S(1)}, u32[]{:S(2)}, u32[]{:S(2)}) collective-permute-start(f32[20,64,128]{2,1,0:T(8,128)S(1)} %multiply_add_fusion.2), channel_id=1, source_target_pairs={{0,4},{4,8},{8,12},{12,16},{16,20},{20,24},{24,28},{28,32},{32,36}... | collective-permute-start | bytes 1966088 | tf_op jit(solution)/shard_map/while/body/eval_jaxpr/ppermute | solution.py:13
  769.0 15.2 %collective-permute-start = (f32[20,64,128]{2,1,0:T(8,128)S(1)}, f32[20,64,128]{2,1,0:T(8,128)S(1)}, u32[]{:S(2)}, u32[]{:S(2)}) collective-permute-start(f32[20,64,128]{2,1,0:T(8,128)S(1)} %multiply_add_fusion.2), channel_id=1, source_target_pairs={{0,4},{4,8},{8,12},{12,16},{16,20},{20,24},{24,28},{28,32},{32,36}... | collective-permute-start | bytes 1966088 | tf_op jit(solution)/shard_map/while/body/eval_jaxpr/ppermute | solution.py:13
  784.2 15.3 %collective-permute-start = (f32[20,64,128]{2,1,0:T(8,128)S(1)}, f32[20,64,128]{2,1,0:T(8,128)S(1)}, u32[]{:S(2)}, u32[]{:S(2)}) collective-permute-start(f32[20,64,128]{2,1,0:T(8,128)S(1)} %multiply_add_fusion.2), channel_id=1, source_target_pairs={{0,4},{4,8},{8,12},{12,16},{16,20},{20,24},{24,28},{28,32},{32,36}... | collective-permute-start | bytes 1966088 | tf_op jit(solution)/shard_map/while/body/eval_jaxpr/ppermute | solution.py:13
  799.7 16.5 %collective-permute-start = (f32[20,64,128]{2,1,0:T(8,128)S(1)}, f32[20,64,128]{2,1,0:T(8,128)S(1)}, u32[]{:S(2)}, u32[]{:S(2)}) collective-permute-start(f32[20,64,128]{2,1,0:T(8,128)S(1)} %multiply_add_fusion.2), channel_id=1, source_target_pairs={{0,4},{4,8},{8,12},{12,16},{16,20},{20,24},{24,28},{28,32},{32,36}... | collective-permute-start | bytes 1966088 | tf_op jit(solution)/shard_map/while/body/eval_jaxpr/ppermute | solution.py:13
  816.3 17.6 %collective-permute-start = (f32[20,64,128]{2,1,0:T(8,128)S(1)}, f32[20,64,128]{2,1,0:T(8,128)S(1)}, u32[]{:S(2)}, u32[]{:S(2)}) collective-permute-start(f32[20,64,128]{2,1,0:T(8,128)S(1)} %multiply_add_fusion.2), channel_id=1, source_target_pairs={{0,4},{4,8},{8,12},{12,16},{16,20},{20,24},{24,28},{28,32},{32,36}... | collective-permute-start | bytes 1966088 | tf_op jit(solution)/shard_map/while/body/eval_jaxpr/ppermute | solution.py:13
  834.1 18.8 %collective-permute-start = (f32[20,64,128]{2,1,0:T(8,128)S(1)}, f32[20,64,128]{2,1,0:T(8,128)S(1)}, u32[]{:S(2)}, u32[]{:S(2)}) collective-permute-start(f32[20,64,128]{2,1,0:T(8,128)S(1)} %multiply_add_fusion.2), channel_id=1, source_target_pairs={{0,4},{4,8},{8,12},{12,16},{16,20},{20,24},{24,28},{28,32},{32,36}... | collective-permute-start | bytes 1966088 | tf_op jit(solution)/shard_map/while/body/eval_jaxpr/ppermute | solution.py:13
  853.0 19.9 %collective-permute-start = (f32[20,64,128]{2,1,0:T(8,128)S(1)}, f32[20,64,128]{2,1,0:T(8,128)S(1)}, u32[]{:S(2)}, u32[]{:S(2)}) collective-permute-start(f32[20,64,128]{2,1,0:T(8,128)S(1)} %multiply_add_fusion.2), channel_id=1, source_target_pairs={{0,4},{4,8},{8,12},{12,16},{16,20},{20,24},{24,28},{28,32},{32,36}... | collective-permute-start | bytes 1966088 | tf_op jit(solution)/shard_map/while/body/eval_jaxpr/ppermute | solution.py:13
  873.1 21.1 %collective-permute-start = (f32[20,64,128]{2,1,0:T(8,128)S(1)}, f32[20,64,128]{2,1,0:T(8,128)S(1)}, u32[]{:S(2)}, u32[]{:S(2)}) collective-permute-start(f32[20,64,128]{2,1,0:T(8,128)S(1)} %multiply_add_fusion.2), channel_id=1, source_target_pairs={{0,4},{4,8},{8,12},{12,16},{16,20},{20,24},{24,28},{28,32},{32,36}... | collective-permute-start | bytes 1966088 | tf_op jit(solution)/shard_map/while/body/eval_jaxpr/ppermute | solution.py:13
  894.3 21.0 %collective-permute-start = (f32[20,64,128]{2,1,0:T(8,128)S(1)}, f32[20,64,128]{2,1,0:T(8,128)S(1)}, u32[]{:S(2)}, u32[]{:S(2)}) collective-permute-start(f32[20,64,128]{2,1,0:T(8,128)S(1)} %multiply_add_fusion.2), channel_id=1, source_target_pairs={{0,4},{4,8},{8,12},{12,16},{16,20},{20,24},{24,28},{28,32},{32,36}... | collective-permute-start | bytes 1966088 | tf_op jit(solution)/shard_map/while/body/eval_jaxpr/ppermute | solution.py:13
  915.4 20.1 %collective-permute-start = (f32[20,64,128]{2,1,0:T(8,128)S(1)}, f32[20,64,128]{2,1,0:T(8,128)S(1)}, u32[]{:S(2)}, u32[]{:S(2)}) collective-permute-start(f32[20,64,128]{2,1,0:T(8,128)S(1)} %multiply_add_fusion.2), channel_id=1, source_target_pairs={{0,4},{4,8},{8,12},{12,16},{16,20},{20,24},{24,28},{28,32},{32,36}... | collective-permute-start | bytes 1966088 | tf_op jit(solution)/shard_map/while/body/eval_jaxpr/ppermute | solution.py:13
  935.7 19.3 %collective-permute-start = (f32[20,64,128]{2,1,0:T(8,128)S(1)}, f32[20,64,128]{2,1,0:T(8,128)S(1)}, u32[]{:S(2)}, u32[]{:S(2)}) collective-permute-start(f32[20,64,128]{2,1,0:T(8,128)S(1)} %multiply_add_fusion.2), channel_id=1, source_target_pairs={{0,4},{4,8},{8,12},{12,16},{16,20},{20,24},{24,28},{28,32},{32,36}... | collective-permute-start | bytes 1966088 | tf_op jit(solution)/shard_map/while/body/eval_jaxpr/ppermute | solution.py:13
  955.1 18.4 %collective-permute-start = (f32[20,64,128]{2,1,0:T(8,128)S(1)}, f32[20,64,128]{2,1,0:T(8,128)S(1)}, u32[]{:S(2)}, u32[]{:S(2)}) collective-permute-start(f32[20,64,128]{2,1,0:T(8,128)S(1)} %multiply_add_fusion.2), channel_id=1, source_target_pairs={{0,4},{4,8},{8,12},{12,16},{16,20},{20,24},{24,28},{28,32},{32,36}... | collective-permute-start | bytes 1966088 | tf_op jit(solution)/shard_map/while/body/eval_jaxpr/ppermute | solution.py:13
  973.7 17.6 %collective-permute-start = (f32[20,64,128]{2,1,0:T(8,128)S(1)}, f32[20,64,128]{2,1,0:T(8,128)S(1)}, u32[]{:S(2)}, u32[]{:S(2)}) collective-permute-start(f32[20,64,128]{2,1,0:T(8,128)S(1)} %multiply_add_fusion.2), channel_id=1, source_target_pairs={{0,4},{4,8},{8,12},{12,16},{16,20},{20,24},{24,28},{28,32},{32,36}... | collective-permute-start | bytes 1966088 | tf_op jit(solution)/shard_map/while/body/eval_jaxpr/ppermute | solution.py:13
  991.4 14.6 %collective-permute-start = (f32[20,64,128]{2,1,0:T(8,128)S(1)}, f32[20,64,128]{2,1,0:T(8,128)S(1)}, u32[]{:S(2)}, u32[]{:S(2)}) collective-permute-start(f32[20,64,128]{2,1,0:T(8,128)S(1)} %multiply_add_fusion.2), channel_id=1, source_target_pairs={{0,4},{4,8},{8,12},{12,16},{16,20},{20,24},{24,28},{28,32},{32,36}... | collective-permute-start | bytes 1966088 | tf_op jit(solution)/shard_map/while/body/eval_jaxpr/ppermute | solution.py:13
  (10 other events, 621.2 us)
Sparse Core Ops, SparseCore 0:
  26.1 36.3 all-gather.1
where the time goes:
time: 1110 us; the launch traced here: 1100 us
  waiting for transfers between devices  556 us (50%)
  local copies, waits for them, and re-layouts  324 us (29%)
  starting transfers between devices  73.4 us (7%)
  matrix products  49.4 us (4%)
  other arithmetic  43.6 us (4%)
  blocking collectives  36.9 us (3%)
  between operations  13.7 us (1%)
    ppermute x32, waiting for transfers between devices, from_behind(): return lax.ppermute(value, axis, pairs)  497 us
    dynamic_update_slice x16, local copies, waits for them, and re-layouts, per_device(): lax.scan(block_terms, start_state, (c_rows.reshape(block_count, SPAN, sta...  251 us
    ppermute x32, starting transfers between devices, from_behind(): return lax.ppermute(value, axis, pairs)  63.7 us
    all_to_all x1, blocking collectives, per_device(): lax.all_to_all(regrouped, 'head', split_axis=0, concat_axis=1, tiled=True)  36.9 us
    all_gather x1, waiting for transfers between devices, per_device(): state_whole = lax.all_gather(state_inputs, 'head', axis=0, tiled=True)  30.6 us
    all_to_all x1, waiting for transfers between devices, per_device(): lax.all_to_all(inner_tokens, 'head', split_axis=1, concat_axis=0, tiled=T...  26.9 us
  transfers between devices with their start and end apart: 35, of which 35 were waited for; matrix products, arithmetic and copies ran while one was open for 2% of the time, Pallas kernels for 0%

commit v1 on v0

--- a/solution.py
+++ b/solution.py
@@ -1,3 +1,4 @@
+import functools
 import jax
 import jax.numpy as jnp
 from jax import lax
@@ -5,6 +6,22 @@
 
 KERNEL = 4
 SPAN = 256
+
+
+def group_patch(z_in, device_axis):
+    inter = jnp.concatenate(
+        jax.lax.all_to_all(
+            jnp.stack(jax.lax.axis_size(device_axis) * [z_in], axis=0),
+            axis_name=device_axis,
+            split_axis=0,
+            concat_axis=0,
+        ),
+        axis=0,
+    )
+    return inter
+
+
+answer_runs = functools.partial(group_patch, device_axis="head")
 
 
 def from_behind(value, axis, by):
@@ -59,7 +76,7 @@
     heads_local = head_rates.shape[1]
     head_width = channels // heads_local
     margin_rows = KERNEL - 1
-    state_whole = lax.all_gather(state_inputs, "head", axis=0, tiled=True)
+    state_whole = answer_runs(state_inputs)
     edge_rows = jnp.concatenate(
         [x_local[context - margin_rows :], state_whole[context - margin_rows :]], axis=1
     )

time: 1110 us -> 1100 us (level)
  between operations: 13.7 us -> 0.31 us
    all_gather x1 -> x0, waiting for transfers between devices: 30.6 us -> none  [per_device(): state_whole = lax.all_gather(state_inputs, 'head', axis=0, tiled=True)]
    all_to_all x1, waiting for transfers between devices: 26.9 us -> 49 us  [per_device(): lax.all_to_all(inner_tokens, 'head', split_axis=1, concat_axis=0, tiled=T...]
  transfers between devices with their start and end apart: 35 -> 34, of which waited for: 35 -> 34; matrix products, arithmetic and copies ran while one was open for 2% -> 2% of each run, Pallas kernels for 0% -> 0%
where the time goes in v1:
time: 1100 us; the launch traced here: 1090 us
  waiting for transfers between devices  553 us (50%)
  local copies, waits for them, and re-layouts  325 us (30%)
  starting transfers between devices  72.4 us (7%)
  matrix products  49.4 us (4%)
  blocking collectives  46.9 us (4%)
  other arithmetic  43.6 us (4%)
    ppermute x32, waiting for transfers between devices, from_behind(): return lax.ppermute(value, axis, pairs)  496 us
    dynamic_update_slice x16, local copies, waits for them, and re-layouts, per_device(): lax.scan(block_terms, start_state, (c_rows.reshape(block_count, SPAN, sta...  251 us
    ppermute x32, starting transfers between devices, from_behind(): return lax.ppermute(value, axis, pairs)  63.7 us
    all_to_all x1, waiting for transfers between devices, per_device(): lax.all_to_all(inner_tokens, 'head', split_axis=1, concat_axis=0, tiled=T...  49 us
    all_to_all x1, blocking collectives, per_device(): lax.all_to_all(regrouped, 'head', split_axis=0, concat_axis=1, tiled=True)  36.9 us
  transfers between devices with their start and end apart: 34, of which 34 were waited for; matrix products, arithmetic and copies ran while one was open for 2% of the time, Pallas kernels for 0%

profile of v1, /device:TPU:6, one launch (start us, length us, event | category | flops | bytes accessed | tf_op | source)
XLA Modules:
  0.0 1092.2 jit_solution(9254635637333386807)
XLA Ops:
  44.7 49.0 %all-to-all-done.1 = bf16[512,4,1280]{2,0,1:T(8,128)(2,1)} async-done(((bf16[512,4,1280]{2,0,1:T(8,128)(2,1)}), bf16[512,4,1280]{2,0,1:T(8,128)(2,1)}, u32[]{:S(2)}, u32[]{:S(2)}) %all-to-all-start.1) | async-done | bytes 5242912 | tf_op jit(solution)/shard_map/all_to_all | solution.py:71
  145.1 307.2 %while.24 = (s32[]{:T(128)}, f32[20,64,128]{2,1,0:T(8,128)S(1)}, f32[8,256,20,64]{1,0,3,2:T(8,128)}, f32[8,256,20]{1,0,2:T(8,128)S(1)}, bf16[8,256,20,64]{1,3,2,...) while((s32[]{:T(128)}, f32[20,64,128]{2,1,0:T(8,128)S(1)}, ...), condition=%wide.region_3.4_spmd.clone, body=%wide.region_0.3_spmd.clone.sunk | while | flops 1199117312 | bytes 13914835 | solution.py:96
  153.7 30.0 %dynamic_update_slice.6 = f32[8,256,20,64]{1,0,3,2:T(8,128)} dynamic-update-slice(f32[8,256,20,64]{1,0,3,2:T(8,128)} %get-tuple-element.251, f32[1,256,20,64]{1,0,3,2:T(1,128)S(1)} %copy.120, s32[]{:T(128)S(6)} %copy.125, s32[]{:T(128)} %constant.36.clone.1..sunk, s32[]{:T(128)} %constant.36.clone.1..sunk, s32[]{:T(128)} %constant.36.clone.1..sunk) | dynamic-update-slice | bytes 2621444 | tf_op jit(solution)/shard_map/while/body/jit(dynamic_update_index_in_dim)/dynamic_update_slice | solution.py:96
  192.1 30.0 %dynamic_update_slice.6 = f32[8,256,20,64]{1,0,3,2:T(8,128)} dynamic-update-slice(f32[8,256,20,64]{1,0,3,2:T(8,128)} %get-tuple-element.251, f32[1,256,20,64]{1,0,3,2:T(1,128)S(1)} %copy.120, s32[]{:T(128)S(6)} %copy.125, s32[]{:T(128)} %constant.36.clone.1..sunk, s32[]{:T(128)} %constant.36.clone.1..sunk, s32[]{:T(128)} %constant.36.clone.1..sunk) | dynamic-update-slice | bytes 2621444 | tf_op jit(solution)/shard_map/while/body/jit(dynamic_update_index_in_dim)/dynamic_update_slice | solution.py:96
  230.5 30.0 %dynamic_update_slice.6 = f32[8,256,20,64]{1,0,3,2:T(8,128)} dynamic-update-slice(f32[8,256,20,64]{1,0,3,2:T(8,128)} %get-tuple-element.251, f32[1,256,20,64]{1,0,3,2:T(1,128)S(1)} %copy.120, s32[]{:T(128)S(6)} %copy.125, s32[]{:T(128)} %constant.36.clone.1..sunk, s32[]{:T(128)} %constant.36.clone.1..sunk, s32[]{:T(128)} %constant.36.clone.1..sunk) | dynamic-update-slice | bytes 2621444 | tf_op jit(solution)/shard_map/while/body/jit(dynamic_update_index_in_dim)/dynamic_update_slice | solution.py:96
  268.8 30.0 %dynamic_update_slice.6 = f32[8,256,20,64]{1,0,3,2:T(8,128)} dynamic-update-slice(f32[8,256,20,64]{1,0,3,2:T(8,128)} %get-tuple-element.251, f32[1,256,20,64]{1,0,3,2:T(1,128)S(1)} %copy.120, s32[]{:T(128)S(6)} %copy.125, s32[]{:T(128)} %constant.36.clone.1..sunk, s32[]{:T(128)} %constant.36.clone.1..sunk, s32[]{:T(128)} %constant.36.clone.1..sunk) | dynamic-update-slice | bytes 2621444 | tf_op jit(solution)/shard_map/while/body/jit(dynamic_update_index_in_dim)/dynamic_update_slice | solution.py:96
  307.2 30.0 %dynamic_update_slice.6 = f32[8,256,20,64]{1,0,3,2:T(8,128)} dynamic-update-slice(f32[8,256,20,64]{1,0,3,2:T(8,128)} %get-tuple-element.251, f32[1,256,20,64]{1,0,3,2:T(1,128)S(1)} %copy.120, s32[]{:T(128)S(6)} %copy.125, s32[]{:T(128)} %constant.36.clone.1..sunk, s32[]{:T(128)} %constant.36.clone.1..sunk, s32[]{:T(128)} %constant.36.clone.1..sunk) | dynamic-update-slice | bytes 2621444 | tf_op jit(solution)/shard_map/while/body/jit(dynamic_update_index_in_dim)/dynamic_update_slice | solution.py:96
  345.6 30.0 %dynamic_update_slice.6 = f32[8,256,20,64]{1,0,3,2:T(8,128)} dynamic-update-slice(f32[8,256,20,64]{1,0,3,2:T(8,128)} %get-tuple-element.251, f32[1,256,20,64]{1,0,3,2:T(1,128)S(1)} %copy.120, s32[]{:T(128)S(6)} %copy.125, s32[]{:T(128)} %constant.36.clone.1..sunk, s32[]{:T(128)} %constant.36.clone.1..sunk, s32[]{:T(128)} %constant.36.clone.1..sunk) | dynamic-update-slice | bytes 2621444 | tf_op jit(solution)/shard_map/while/body/jit(dynamic_update_index_in_dim)/dynamic_update_slice | solution.py:96
  383.9 30.0 %dynamic_update_slice.6 = f32[8,256,20,64]{1,0,3,2:T(8,128)} dynamic-update-slice(f32[8,256,20,64]{1,0,3,2:T(8,128)} %get-tuple-element.251, f32[1,256,20,64]{1,0,3,2:T(1,128)S(1)} %copy.120, s32[]{:T(128)S(6)} %copy.125, s32[]{:T(128)} %constant.36.clone.1..sunk, s32[]{:T(128)} %constant.36.clone.1..sunk, s32[]{:T(128)} %constant.36.clone.1..sunk) | dynamic-update-slice | bytes 2621444 | tf_op jit(solution)/shard_map/while/body/jit(dynamic_update_index_in_dim)/dynamic_update_slice | solution.py:96
  422.3 30.0 %dynamic_update_slice.6 = f32[8,256,20,64]{1,0,3,2:T(8,128)} dynamic-update-slice(f32[8,256,20,64]{1,0,3,2:T(8,128)} %get-tuple-element.251, f32[1,256,20,64]{1,0,3,2:T(1,128)S(1)} %copy.120, s32[]{:T(128)S(6)} %copy.125, s32[]{:T(128)} %constant.36.clone.1..sunk, s32[]{:T(128)} %constant.36.clone.1..sunk, s32[]{:T(128)} %constant.36.clone.1..sunk) | dynamic-update-slice | bytes 2621444 | tf_op jit(solution)/shard_map/while/body/jit(dynamic_update_index_in_dim)/dynamic_update_slice | solution.py:96
  463.8 557.4 %while.23 = (s32[]{:T(128)}, f32[20,64,128]{2,1,0:T(8,128)S(1)}, f32[20]{0:T(128)S(1)}, f32[20,64,128]{2,1,0:T(8,128)S(1)}, s32[]{:T(128)}) while((s32[]{:T(128)}, f32[20,64,128]{2,1,0:T(8,128)S(1)}, f32[20]{0:T(128)S(1)}, f32[20,64,128]{2,1,0:T(8,128)S(1)}, s32[]{:T(128)}) %tuple.57), condition=%wide.region_7.8_spmd, body=%wide.region_6.7_spmd.sunk | while | flops 327682 | bytes 4587701 | solution.py:112
  529.2 15.0 %collective-permute-done = f32[20,64,128]{2,1,0:T(8,128)S(1)} collective-permute-done((f32[20,64,128]{2,1,0:T(8,128)S(1)}, f32[20,64,128]{2,1,0:T(8,128)S(1)}, u32[]{:S(2)}, u32[]{:S(2)}) %collective-permute-start) | collective-permute-done | bytes 655392 | tf_op jit(solution)/shard_map/while/body/eval_jaxpr/ppermute | solution.py:30
  546.2 16.1 %collective-permute-done = f32[20,64,128]{2,1,0:T(8,128)S(1)} collective-permute-done((f32[20,64,128]{2,1,0:T(8,128)S(1)}, f32[20,64,128]{2,1,0:T(8,128)S(1)}, u32[]{:S(2)}, u32[]{:S(2)}) %collective-permute-start) | collective-permute-done | bytes 655392 | tf_op jit(solution)/shard_map/while/body/eval_jaxpr/ppermute | solution.py:30
  564.4 17.3 %collective-permute-done = f32[20,64,128]{2,1,0:T(8,128)S(1)} collective-permute-done((f32[20,64,128]{2,1,0:T(8,128)S(1)}, f32[20,64,128]{2,1,0:T(8,128)S(1)}, u32[]{:S(2)}, u32[]{:S(2)}) %collective-permute-start) | collective-permute-done | bytes 655392 | tf_op jit(solution)/shard_map/while/body/eval_jaxpr/ppermute | solution.py:30
  583.7 18.4 %collective-permute-done = f32[20,64,128]{2,1,0:T(8,128)S(1)} collective-permute-done((f32[20,64,128]{2,1,0:T(8,128)S(1)}, f32[20,64,128]{2,1,0:T(8,128)S(1)}, u32[]{:S(2)}, u32[]{:S(2)}) %collective-permute-start) | collective-permute-done | bytes 655392 | tf_op jit(solution)/shard_map/while/body/eval_jaxpr/ppermute | solution.py:30
  604.2 19.6 %collective-permute-done = f32[20,64,128]{2,1,0:T(8,128)S(1)} collective-permute-done((f32[20,64,128]{2,1,0:T(8,128)S(1)}, f32[20,64,128]{2,1,0:T(8,128)S(1)}, u32[]{:S(2)}, u32[]{:S(2)}) %collective-permute-start) | collective-permute-done | bytes 655392 | tf_op jit(solution)/shard_map/while/body/eval_jaxpr/ppermute | solution.py:30
  625.8 18.8 %collective-permute-done = f32[20,64,128]{2,1,0:T(8,128)S(1)} collective-permute-done((f32[20,64,128]{2,1,0:T(8,128)S(1)}, f32[20,64,128]{2,1,0:T(8,128)S(1)}, u32[]{:S(2)}, u32[]{:S(2)}) %collective-permute-start) | collective-permute-done | bytes 655392 | tf_op jit(solution)/shard_map/while/body/eval_jaxpr/ppermute | solution.py:30
  646.7 18.0 %collective-permute-done = f32[20,64,128]{2,1,0:T(8,128)S(1)} collective-permute-done((f32[20,64,128]{2,1,0:T(8,128)S(1)}, f32[20,64,128]{2,1,0:T(8,128)S(1)}, u32[]{:S(2)}, u32[]{:S(2)}) %collective-permute-start) | collective-permute-done | bytes 655392 | tf_op jit(solution)/shard_map/while/body/eval_jaxpr/ppermute | solution.py:30
  666.7 17.1 %collective-permute-done = f32[20,64,128]{2,1,0:T(8,128)S(1)} collective-permute-done((f32[20,64,128]{2,1,0:T(8,128)S(1)}, f32[20,64,128]{2,1,0:T(8,128)S(1)}, u32[]{:S(2)}, u32[]{:S(2)}) %collective-permute-start) | collective-permute-done | bytes 655392 | tf_op jit(solution)/shard_map/while/body/eval_jaxpr/ppermute | solution.py:30
  685.9 16.3 %collective-permute-done = f32[20,64,128]{2,1,0:T(8,128)S(1)} collective-permute-done((f32[20,64,128]{2,1,0:T(8,128)S(1)}, f32[20,64,128]{2,1,0:T(8,128)S(1)}, u32[]{:S(2)}, u32[]{:S(2)}) %collective-permute-start) | collective-permute-done | bytes 655392 | tf_op jit(solution)/shard_map/while/body/eval_jaxpr/ppermute | solution.py:30
  704.2 15.4 %collective-permute-done = f32[20,64,128]{2,1,0:T(8,128)S(1)} collective-permute-done((f32[20,64,128]{2,1,0:T(8,128)S(1)}, f32[20,64,128]{2,1,0:T(8,128)S(1)}, u32[]{:S(2)}, u32[]{:S(2)}) %collective-permute-start) | collective-permute-done | bytes 655392 | tf_op jit(solution)/shard_map/while/body/eval_jaxpr/ppermute | solution.py:30
  784.8 14.9 %collective-permute-done = f32[20,64,128]{2,1,0:T(8,128)S(1)} collective-permute-done((f32[20,64,128]{2,1,0:T(8,128)S(1)}, f32[20,64,128]{2,1,0:T(8,128)S(1)}, u32[]{:S(2)}, u32[]{:S(2)}) %collective-permute-start) | collective-permute-done | bytes 655392 | tf_op jit(solution)/shard_map/while/body/eval_jaxpr/ppermute | solution.py:30
  801.8 16.1 %collective-permute-done = f32[20,64,128]{2,1,0:T(8,128)S(1)} collective-permute-done((f32[20,64,128]{2,1,0:T(8,128)S(1)}, f32[20,64,128]{2,1,0:T(8,128)S(1)}, u32[]{:S(2)}, u32[]{:S(2)}) %collective-permute-start) | collective-permute-done | bytes 655392 | tf_op jit(solution)/shard_map/while/body/eval_jaxpr/ppermute | solution.py:30
  820.0 17.2 %collective-permute-done = f32[20,64,128]{2,1,0:T(8,128)S(1)} collective-permute-done((f32[20,64,128]{2,1,0:T(8,128)S(1)}, f32[20,64,128]{2,1,0:T(8,128)S(1)}, u32[]{:S(2)}, u32[]{:S(2)}) %collective-permute-start) | collective-permute-done | bytes 655392 | tf_op jit(solution)/shard_map/while/body/eval_jaxpr/ppermute | solution.py:30
  839.3 18.4 %collective-permute-done = f32[20,64,128]{2,1,0:T(8,128)S(1)} collective-permute-done((f32[20,64,128]{2,1,0:T(8,128)S(1)}, f32[20,64,128]{2,1,0:T(8,128)S(1)}, u32[]{:S(2)}, u32[]{:S(2)}) %collective-permute-start) | collective-permute-done | bytes 655392 | tf_op jit(solution)/shard_map/while/body/eval_jaxpr/ppermute | solution.py:30
  859.8 19.5 %collective-permute-done = f32[20,64,128]{2,1,0:T(8,128)S(1)} collective-permute-done((f32[20,64,128]{2,1,0:T(8,128)S(1)}, f32[20,64,128]{2,1,0:T(8,128)S(1)}, u32[]{:S(2)}, u32[]{:S(2)}) %collective-permute-start) | collective-permute-done | bytes 655392 | tf_op jit(solution)/shard_map/while/body/eval_jaxpr/ppermute | solution.py:30
  881.4 18.8 %collective-permute-done = f32[20,64,128]{2,1,0:T(8,128)S(1)} collective-permute-done((f32[20,64,128]{2,1,0:T(8,128)S(1)}, f32[20,64,128]{2,1,0:T(8,128)S(1)}, u32[]{:S(2)}, u32[]{:S(2)}) %collective-permute-start) | collective-permute-done | bytes 655392 | tf_op jit(solution)/shard_map/while/body/eval_jaxpr/ppermute | solution.py:30
  902.3 18.0 %collective-permute-done = f32[20,64,128]{2,1,0:T(8,128)S(1)} collective-permute-done((f32[20,64,128]{2,1,0:T(8,128)S(1)}, f32[20,64,128]{2,1,0:T(8,128)S(1)}, u32[]{:S(2)}, u32[]{:S(2)}) %collective-permute-start) | collective-permute-done | bytes 655392 | tf_op jit(solution)/shard_map/while/body/eval_jaxpr/ppermute | solution.py:30
  922.3 17.1 %collective-permute-done = f32[20,64,128]{2,1,0:T(8,128)S(1)} collective-permute-done((f32[20,64,128]{2,1,0:T(8,128)S(1)}, f32[20,64,128]{2,1,0:T(8,128)S(1)}, u32[]{:S(2)}, u32[]{:S(2)}) %collective-permute-start) | collective-permute-done | bytes 655392 | tf_op jit(solution)/shard_map/while/body/eval_jaxpr/ppermute | solution.py:30
  941.5 16.3 %collective-permute-done = f32[20,64,128]{2,1,0:T(8,128)S(1)} collective-permute-done((f32[20,64,128]{2,1,0:T(8,128)S(1)}, f32[20,64,128]{2,1,0:T(8,128)S(1)}, u32[]{:S(2)}, u32[]{:S(2)}) %collective-permute-start) | collective-permute-done | bytes 655392 | tf_op jit(solution)/shard_map/while/body/eval_jaxpr/ppermute | solution.py:30
  959.8 15.4 %collective-permute-done = f32[20,64,128]{2,1,0:T(8,128)S(1)} collective-permute-done((f32[20,64,128]{2,1,0:T(8,128)S(1)}, f32[20,64,128]{2,1,0:T(8,128)S(1)}, u32[]{:S(2)}, u32[]{:S(2)}) %collective-permute-start) | collective-permute-done | bytes 655392 | tf_op jit(solution)/shard_map/while/body/eval_jaxpr/ppermute | solution.py:30
  1047.4 36.9 %all_to_all.57 = bf16[4,512,1280]{1,2,0:T(8,128)(2,1)} all-to-all(bf16[4,512,1280]{1,2,0:T(8,128)(2,1)S(1)} %copy.91), channel_id=1, replica_groups=mesh['run'=2,'ctx'=32,'head'=4] {'head'}, dimensions={0} | all-to-all | bytes 10485760 | tf_op jit(solution)/shard_map/all_to_all | solution.py:122
  (311 shorter events, 420.4 us)
Async XLA Ops:
  13.0 17.4 %all-to-all-start.2 = ((bf16[4,512,256]{2,1,0:T(8,128)(2,1)}), bf16[4,512,256]{2,1,0:T(8,128)(2,1)S(1)}, u32[]{:S(2)}, u32[]{:S(2)}) async-start(bf16[4,512,256]{2,1,0:T(8,128)(2,1)} %stack.2), calls=%async_computation.2 | async-start | bytes 2097152 | tf_op jit(solution)/shard_map/all_to_all | solution.py:13
  30.4 63.3 %all-to-all-start.1 = ((bf16[512,4,1280]{2,0,1:T(8,128)(2,1)}), bf16[512,4,1280]{2,0,1:T(8,128)(2,1)}, u32[]{:S(2)}, u32[]{:S(2)}) async-start(bf16[512,4,1280]{2,0,1:T(8,128)(2,1)} %bitcast.131), calls=%async_computation.1 | async-start | bytes 10485760 | tf_op jit(solution)/shard_map/all_to_all | solution.py:71
  464.0 16.6 %collective-permute-start = (f32[20,64,128]{2,1,0:T(8,128)S(1)}, f32[20,64,128]{2,1,0:T(8,128)S(1)}, u32[]{:S(2)}, u32[]{:S(2)}) collective-permute-start(f32[20,64,128]{2,1,0:T(8,128)S(1)} %multiply_add_fusion.2), channel_id=1, source_target_pairs={{0,4},{4,8},{8,12},{12,16},{16,20},{20,24},{24,28},{28,32},{32,36}... | collective-permute-start | bytes 1966088 | tf_op jit(solution)/shard_map/while/body/eval_jaxpr/ppermute | solution.py:30
  480.7 15.6 %collective-permute-start = (f32[20,64,128]{2,1,0:T(8,128)S(1)}, f32[20,64,128]{2,1,0:T(8,128)S(1)}, u32[]{:S(2)}, u32[]{:S(2)}) collective-permute-start(f32[20,64,128]{2,1,0:T(8,128)S(1)} %multiply_add_fusion.2), channel_id=1, source_target_pairs={{0,4},{4,8},{8,12},{12,16},{16,20},{20,24},{24,28},{28,32},{32,36}... | collective-permute-start | bytes 1966088 | tf_op jit(solution)/shard_map/while/body/eval_jaxpr/ppermute | solution.py:30
  496.5 14.8 %collective-permute-start = (f32[20,64,128]{2,1,0:T(8,128)S(1)}, f32[20,64,128]{2,1,0:T(8,128)S(1)}, u32[]{:S(2)}, u32[]{:S(2)}) collective-permute-start(f32[20,64,128]{2,1,0:T(8,128)S(1)} %multiply_add_fusion.2), channel_id=1, source_target_pairs={{0,4},{4,8},{8,12},{12,16},{16,20},{20,24},{24,28},{28,32},{32,36}... | collective-permute-start | bytes 1966088 | tf_op jit(solution)/shard_map/while/body/eval_jaxpr/ppermute | solution.py:30
  511.4 15.8 %collective-permute-start = (f32[20,64,128]{2,1,0:T(8,128)S(1)}, f32[20,64,128]{2,1,0:T(8,128)S(1)}, u32[]{:S(2)}, u32[]{:S(2)}) collective-permute-start(f32[20,64,128]{2,1,0:T(8,128)S(1)} %multiply_add_fusion.2), channel_id=1, source_target_pairs={{0,4},{4,8},{8,12},{12,16},{16,20},{20,24},{24,28},{28,32},{32,36}... | collective-permute-start | bytes 1966088 | tf_op jit(solution)/shard_map/while/body/eval_jaxpr/ppermute | solution.py:30
  527.2 16.9 %collective-permute-start = (f32[20,64,128]{2,1,0:T(8,128)S(1)}, f32[20,64,128]{2,1,0:T(8,128)S(1)}, u32[]{:S(2)}, u32[]{:S(2)}) collective-permute-start(f32[20,64,128]{2,1,0:T(8,128)S(1)} %multiply_add_fusion.2), channel_id=1, source_target_pairs={{0,4},{4,8},{8,12},{12,16},{16,20},{20,24},{24,28},{28,32},{32,36}... | collective-permute-start | bytes 1966088 | tf_op jit(solution)/shard_map/while/body/eval_jaxpr/ppermute | solution.py:30
  544.3 18.0 %collective-permute-start = (f32[20,64,128]{2,1,0:T(8,128)S(1)}, f32[20,64,128]{2,1,0:T(8,128)S(1)}, u32[]{:S(2)}, u32[]{:S(2)}) collective-permute-start(f32[20,64,128]{2,1,0:T(8,128)S(1)} %multiply_add_fusion.2), channel_id=1, source_target_pairs={{0,4},{4,8},{8,12},{12,16},{16,20},{20,24},{24,28},{28,32},{32,36}... | collective-permute-start | bytes 1966088 | tf_op jit(solution)/shard_map/while/body/eval_jaxpr/ppermute | solution.py:30
  562.4 19.2 %collective-permute-start = (f32[20,64,128]{2,1,0:T(8,128)S(1)}, f32[20,64,128]{2,1,0:T(8,128)S(1)}, u32[]{:S(2)}, u32[]{:S(2)}) collective-permute-start(f32[20,64,128]{2,1,0:T(8,128)S(1)} %multiply_add_fusion.2), channel_id=1, source_target_pairs={{0,4},{4,8},{8,12},{12,16},{16,20},{20,24},{24,28},{28,32},{32,36}... | collective-permute-start | bytes 1966088 | tf_op jit(solution)/shard_map/while/body/eval_jaxpr/ppermute | solution.py:30
  581.8 20.3 %collective-permute-start = (f32[20,64,128]{2,1,0:T(8,128)S(1)}, f32[20,64,128]{2,1,0:T(8,128)S(1)}, u32[]{:S(2)}, u32[]{:S(2)}) collective-permute-start(f32[20,64,128]{2,1,0:T(8,128)S(1)} %multiply_add_fusion.2), channel_id=1, source_target_pairs={{0,4},{4,8},{8,12},{12,16},{16,20},{20,24},{24,28},{28,32},{32,36}... | collective-permute-start | bytes 1966088 | tf_op jit(solution)/shard_map/while/body/eval_jaxpr/ppermute | solution.py:30
  602.2 21.5 %collective-permute-start = (f32[20,64,128]{2,1,0:T(8,128)S(1)}, f32[20,64,128]{2,1,0:T(8,128)S(1)}, u32[]{:S(2)}, u32[]{:S(2)}) collective-permute-start(f32[20,64,128]{2,1,0:T(8,128)S(1)} %multiply_add_fusion.2), channel_id=1, source_target_pairs={{0,4},{4,8},{8,12},{12,16},{16,20},{20,24},{24,28},{28,32},{32,36}... | collective-permute-start | bytes 1966088 | tf_op jit(solution)/shard_map/while/body/eval_jaxpr/ppermute | solution.py:30
  623.9 20.8 %collective-permute-start = (f32[20,64,128]{2,1,0:T(8,128)S(1)}, f32[20,64,128]{2,1,0:T(8,128)S(1)}, u32[]{:S(2)}, u32[]{:S(2)}) collective-permute-start(f32[20,64,128]{2,1,0:T(8,128)S(1)} %multiply_add_fusion.2), channel_id=1, source_target_pairs={{0,4},{4,8},{8,12},{12,16},{16,20},{20,24},{24,28},{28,32},{32,36}... | collective-permute-start | bytes 1966088 | tf_op jit(solution)/shard_map/while/body/eval_jaxpr/ppermute | solution.py:30
  644.8 19.9 %collective-permute-start = (f32[20,64,128]{2,1,0:T(8,128)S(1)}, f32[20,64,128]{2,1,0:T(8,128)S(1)}, u32[]{:S(2)}, u32[]{:S(2)}) collective-permute-start(f32[20,64,128]{2,1,0:T(8,128)S(1)} %multiply_add_fusion.2), channel_id=1, source_target_pairs={{0,4},{4,8},{8,12},{12,16},{16,20},{20,24},{24,28},{28,32},{32,36}... | collective-permute-start | bytes 1966088 | tf_op jit(solution)/shard_map/while/body/eval_jaxpr/ppermute | solution.py:30
  664.8 19.0 %collective-permute-start = (f32[20,64,128]{2,1,0:T(8,128)S(1)}, f32[20,64,128]{2,1,0:T(8,128)S(1)}, u32[]{:S(2)}, u32[]{:S(2)}) collective-permute-start(f32[20,64,128]{2,1,0:T(8,128)S(1)} %multiply_add_fusion.2), channel_id=1, source_target_pairs={{0,4},{4,8},{8,12},{12,16},{16,20},{20,24},{24,28},{28,32},{32,36}... | collective-permute-start | bytes 1966088 | tf_op jit(solution)/shard_map/while/body/eval_jaxpr/ppermute | solution.py:30
  684.0 18.2 %collective-permute-start = (f32[20,64,128]{2,1,0:T(8,128)S(1)}, f32[20,64,128]{2,1,0:T(8,128)S(1)}, u32[]{:S(2)}, u32[]{:S(2)}) collective-permute-start(f32[20,64,128]{2,1,0:T(8,128)S(1)} %multiply_add_fusion.2), channel_id=1, source_target_pairs={{0,4},{4,8},{8,12},{12,16},{16,20},{20,24},{24,28},{28,32},{32,36}... | collective-permute-start | bytes 1966088 | tf_op jit(solution)/shard_map/while/body/eval_jaxpr/ppermute | solution.py:30
  702.3 17.3 %collective-permute-start = (f32[20,64,128]{2,1,0:T(8,128)S(1)}, f32[20,64,128]{2,1,0:T(8,128)S(1)}, u32[]{:S(2)}, u32[]{:S(2)}) collective-permute-start(f32[20,64,128]{2,1,0:T(8,128)S(1)} %multiply_add_fusion.2), channel_id=1, source_target_pairs={{0,4},{4,8},{8,12},{12,16},{16,20},{20,24},{24,28},{28,32},{32,36}... | collective-permute-start | bytes 1966088 | tf_op jit(solution)/shard_map/while/body/eval_jaxpr/ppermute | solution.py:30
  719.8 16.5 %collective-permute-start = (f32[20,64,128]{2,1,0:T(8,128)S(1)}, f32[20,64,128]{2,1,0:T(8,128)S(1)}, u32[]{:S(2)}, u32[]{:S(2)}) collective-permute-start(f32[20,64,128]{2,1,0:T(8,128)S(1)} %multiply_add_fusion.2), channel_id=1, source_target_pairs={{0,4},{4,8},{8,12},{12,16},{16,20},{20,24},{24,28},{28,32},{32,36}... | collective-permute-start | bytes 1966088 | tf_op jit(solution)/shard_map/while/body/eval_jaxpr/ppermute | solution.py:30
  736.4 15.6 %collective-permute-start = (f32[20,64,128]{2,1,0:T(8,128)S(1)}, f32[20,64,128]{2,1,0:T(8,128)S(1)}, u32[]{:S(2)}, u32[]{:S(2)}) collective-permute-start(f32[20,64,128]{2,1,0:T(8,128)S(1)} %multiply_add_fusion.2), channel_id=1, source_target_pairs={{0,4},{4,8},{8,12},{12,16},{16,20},{20,24},{24,28},{28,32},{32,36}... | collective-permute-start | bytes 1966088 | tf_op jit(solution)/shard_map/while/body/eval_jaxpr/ppermute | solution.py:30
  752.1 14.8 %collective-permute-start = (f32[20,64,128]{2,1,0:T(8,128)S(1)}, f32[20,64,128]{2,1,0:T(8,128)S(1)}, u32[]{:S(2)}, u32[]{:S(2)}) collective-permute-start(f32[20,64,128]{2,1,0:T(8,128)S(1)} %multiply_add_fusion.2), channel_id=1, source_target_pairs={{0,4},{4,8},{8,12},{12,16},{16,20},{20,24},{24,28},{28,32},{32,36}... | collective-permute-start | bytes 1966088 | tf_op jit(solution)/shard_map/while/body/eval_jaxpr/ppermute | solution.py:30
  767.0 15.7 %collective-permute-start = (f32[20,64,128]{2,1,0:T(8,128)S(1)}, f32[20,64,128]{2,1,0:T(8,128)S(1)}, u32[]{:S(2)}, u32[]{:S(2)}) collective-permute-start(f32[20,64,128]{2,1,0:T(8,128)S(1)} %multiply_add_fusion.2), channel_id=1, source_target_pairs={{0,4},{4,8},{8,12},{12,16},{16,20},{20,24},{24,28},{28,32},{32,36}... | collective-permute-start | bytes 1966088 | tf_op jit(solution)/shard_map/while/body/eval_jaxpr/ppermute | solution.py:30
  782.9 16.9 %collective-permute-start = (f32[20,64,128]{2,1,0:T(8,128)S(1)}, f32[20,64,128]{2,1,0:T(8,128)S(1)}, u32[]{:S(2)}, u32[]{:S(2)}) collective-permute-start(f32[20,64,128]{2,1,0:T(8,128)S(1)} %multiply_add_fusion.2), channel_id=1, source_target_pairs={{0,4},{4,8},{8,12},{12,16},{16,20},{20,24},{24,28},{28,32},{32,36}... | collective-permute-start | bytes 1966088 | tf_op jit(solution)/shard_map/while/body/eval_jaxpr/ppermute | solution.py:30
  799.9 18.0 %collective-permute-start = (f32[20,64,128]{2,1,0:T(8,128)S(1)}, f32[20,64,128]{2,1,0:T(8,128)S(1)}, u32[]{:S(2)}, u32[]{:S(2)}) collective-permute-start(f32[20,64,128]{2,1,0:T(8,128)S(1)} %multiply_add_fusion.2), channel_id=1, source_target_pairs={{0,4},{4,8},{8,12},{12,16},{16,20},{20,24},{24,28},{28,32},{32,36}... | collective-permute-start | bytes 1966088 | tf_op jit(solution)/shard_map/while/body/eval_jaxpr/ppermute | solution.py:30
  818.1 19.2 %collective-permute-start = (f32[20,64,128]{2,1,0:T(8,128)S(1)}, f32[20,64,128]{2,1,0:T(8,128)S(1)}, u32[]{:S(2)}, u32[]{:S(2)}) collective-permute-start(f32[20,64,128]{2,1,0:T(8,128)S(1)} %multiply_add_fusion.2), channel_id=1, source_target_pairs={{0,4},{4,8},{8,12},{12,16},{16,20},{20,24},{24,28},{28,32},{32,36}... | collective-permute-start | bytes 1966088 | tf_op jit(solution)/shard_map/while/body/eval_jaxpr/ppermute | solution.py:30
  837.4 20.3 %collective-permute-start = (f32[20,64,128]{2,1,0:T(8,128)S(1)}, f32[20,64,128]{2,1,0:T(8,128)S(1)}, u32[]{:S(2)}, u32[]{:S(2)}) collective-permute-start(f32[20,64,128]{2,1,0:T(8,128)S(1)} %multiply_add_fusion.2), channel_id=1, source_target_pairs={{0,4},{4,8},{8,12},{12,16},{16,20},{20,24},{24,28},{28,32},{32,36}... | collective-permute-start | bytes 1966088 | tf_op jit(solution)/shard_map/while/body/eval_jaxpr/ppermute | solution.py:30
  857.8 21.5 %collective-permute-start = (f32[20,64,128]{2,1,0:T(8,128)S(1)}, f32[20,64,128]{2,1,0:T(8,128)S(1)}, u32[]{:S(2)}, u32[]{:S(2)}) collective-permute-start(f32[20,64,128]{2,1,0:T(8,128)S(1)} %multiply_add_fusion.2), channel_id=1, source_target_pairs={{0,4},{4,8},{8,12},{12,16},{16,20},{20,24},{24,28},{28,32},{32,36}... | collective-permute-start | bytes 1966088 | tf_op jit(solution)/shard_map/while/body/eval_jaxpr/ppermute | solution.py:30
  879.4 20.8 %collective-permute-start = (f32[20,64,128]{2,1,0:T(8,128)S(1)}, f32[20,64,128]{2,1,0:T(8,128)S(1)}, u32[]{:S(2)}, u32[]{:S(2)}) collective-permute-start(f32[20,64,128]{2,1,0:T(8,128)S(1)} %multiply_add_fusion.2), channel_id=1, source_target_pairs={{0,4},{4,8},{8,12},{12,16},{16,20},{20,24},{24,28},{28,32},{32,36}... | collective-permute-start | bytes 1966088 | tf_op jit(solution)/shard_map/while/body/eval_jaxpr/ppermute | solution.py:30
  900.3 19.9 %collective-permute-start = (f32[20,64,128]{2,1,0:T(8,128)S(1)}, f32[20,64,128]{2,1,0:T(8,128)S(1)}, u32[]{:S(2)}, u32[]{:S(2)}) collective-permute-start(f32[20,64,128]{2,1,0:T(8,128)S(1)} %multiply_add_fusion.2), channel_id=1, source_target_pairs={{0,4},{4,8},{8,12},{12,16},{16,20},{20,24},{24,28},{28,32},{32,36}... | collective-permute-start | bytes 1966088 | tf_op jit(solution)/shard_map/while/body/eval_jaxpr/ppermute | solution.py:30
  920.4 19.0 %collective-permute-start = (f32[20,64,128]{2,1,0:T(8,128)S(1)}, f32[20,64,128]{2,1,0:T(8,128)S(1)}, u32[]{:S(2)}, u32[]{:S(2)}) collective-permute-start(f32[20,64,128]{2,1,0:T(8,128)S(1)} %multiply_add_fusion.2), channel_id=1, source_target_pairs={{0,4},{4,8},{8,12},{12,16},{16,20},{20,24},{24,28},{28,32},{32,36}... | collective-permute-start | bytes 1966088 | tf_op jit(solution)/shard_map/while/body/eval_jaxpr/ppermute | solution.py:30
  939.5 18.2 %collective-permute-start = (f32[20,64,128]{2,1,0:T(8,128)S(1)}, f32[20,64,128]{2,1,0:T(8,128)S(1)}, u32[]{:S(2)}, u32[]{:S(2)}) collective-permute-start(f32[20,64,128]{2,1,0:T(8,128)S(1)} %multiply_add_fusion.2), channel_id=1, source_target_pairs={{0,4},{4,8},{8,12},{12,16},{16,20},{20,24},{24,28},{28,32},{32,36}... | collective-permute-start | bytes 1966088 | tf_op jit(solution)/shard_map/while/body/eval_jaxpr/ppermute | solution.py:30
  957.9 17.3 %collective-permute-start = (f32[20,64,128]{2,1,0:T(8,128)S(1)}, f32[20,64,128]{2,1,0:T(8,128)S(1)}, u32[]{:S(2)}, u32[]{:S(2)}) collective-permute-start(f32[20,64,128]{2,1,0:T(8,128)S(1)} %multiply_add_fusion.2), channel_id=1, source_target_pairs={{0,4},{4,8},{8,12},{12,16},{16,20},{20,24},{24,28},{28,32},{32,36}... | collective-permute-start | bytes 1966088 | tf_op jit(solution)/shard_map/while/body/eval_jaxpr/ppermute | solution.py:30
  975.3 16.5 %collective-permute-start = (f32[20,64,128]{2,1,0:T(8,128)S(1)}, f32[20,64,128]{2,1,0:T(8,128)S(1)}, u32[]{:S(2)}, u32[]{:S(2)}) collective-permute-start(f32[20,64,128]{2,1,0:T(8,128)S(1)} %multiply_add_fusion.2), channel_id=1, source_target_pairs={{0,4},{4,8},{8,12},{12,16},{16,20},{20,24},{24,28},{28,32},{32,36}... | collective-permute-start | bytes 1966088 | tf_op jit(solution)/shard_map/while/body/eval_jaxpr/ppermute | solution.py:30
  1006.7 14.6 %collective-permute-start = (f32[20,64,128]{2,1,0:T(8,128)S(1)}, f32[20,64,128]{2,1,0:T(8,128)S(1)}, u32[]{:S(2)}, u32[]{:S(2)}) collective-permute-start(f32[20,64,128]{2,1,0:T(8,128)S(1)} %multiply_add_fusion.2), channel_id=1, source_target_pairs={{0,4},{4,8},{8,12},{12,16},{16,20},{20,24},{24,28},{28,32},{32,36}... | collective-permute-start | bytes 1966088 | tf_op jit(solution)/shard_map/while/body/eval_jaxpr/ppermute | solution.py:30
  (10 other events, 620.0 us)
